TPU v7x, 128 devices: a whole 4x4x4 slice. The times are simulated.
128 devices in a mesh: tok: 8 (over z, y_hi), head: 16 (over x, y_lo, core).
Axes of the slice: x: 4, y: 4 (y_hi: 2, y_lo: 2; y = y_hi * 2 + y_lo), z: 4, core: 2. Of those that a mesh axis runs over, the one named last changes fastest.
Arguments:
- states: bfloat16 [4096, 4096], P('tok', 'head'), may hold values from -400 to 400
- pre_gain: float32 [4096], replicated, may hold values from 0.5 to 1.5
- pre_shift: float32 [4096], replicated, may hold values from -1.75 to 1.75
- mlp_gain: float32 [4096], replicated, may hold values from 0.5 to 1.5
- mlp_shift: float32 [4096], replicated, may hold values from -1.75 to 1.75
- qkv_weight: bfloat16 [4096, 12288], P('tok', 'head'), may hold values from -0.09375 to 0.09375
- qkv_bias: float32 [12288], P('head'), may hold values from -1.75 to 1.75
- out_weight: bfloat16 [4096, 4096], P('head', 'tok'), may hold values from -0.125 to 0.125
- out_bias: float32 [4096], P('head'), may hold values from -1.75 to 1.75
- up_weight: bfloat16 [4096, 16384], P(None, 'head'), may hold values from -0.09375 to 0.09375
- up_bias: float32 [16384], P('head'), may hold values from -1.75 to 1.75
- down_weight: bfloat16 [16384, 4096], P('head'), may hold values from -0.0625 to 0.0625
- down_bias: float32 [4096], P('head'), may hold values from -1.75 to 1.75
- kv_cache: bfloat16 [1152, 2, 16, 4096], P(('tok', 'head')), may hold values from -320 to 320, as said below
- token_request: int32 [4096], P('tok'), may hold values from 0 to 15, as said below
- cached_len: int32 [16], P('tok'), may hold values from 128 to 1024, as said below
- page_table: int32 [16, 64], P('tok'), may hold values from 0 to 143, as said below
- migrations: int32 [64, 2], P('tok'), may hold values from 0 to 143, as said below
Outputs:
- update: bfloat16 [4096, 4096], P('tok', 'head')
Inputs may be any that keep to these rules, and one draw needn't show every extreme that they name: `token_request`: ids never fall; the tokens of request r lie among tokens (r // 2) * 512 to that plus 512 - 1, and every request has one token or more. `cached_len`: some request holds exactly 1024. `page_table`: the entries of one block are distinct. `migrations`: targets of one block are distinct and none is also a source of that block. `kv_cache`: keys are stored already rotated.
All inputs are finite; a program needn't handle non-finite values.
Results may differ from a plain program's by a relative error of at most 0.018.
The roundings to bfloat16 on the way count: a program that leaves them out, or rounds other values in their place, can miss the bound.
Values may be sent and summed in bfloat16 or wider, within the bound.
No kernel may reach another device: no remote copies, remote signals or barrier semaphores. Data moves between devices by JAX's collectives and lax.ppermute only.
A program may use at most 128 MiB of HBM per device.

v0:
```python
import jax
import jax.numpy as jnp
from jax import lax
from jax.sharding import PartitionSpec as P

HD = 128
ROT = 32
epsilon = 1e-05


def layer_norm(wide, gain, shift):
    row_mean = jnp.mean(wide, axis=1, keepdims=True)
    centred = wide - row_mean
    row_var = jnp.mean(centred * centred, axis=1, keepdims=True)
    return (centred * lax.rsqrt(row_var + epsilon) * gain + shift).astype(jnp.bfloat16)


def rotate(vectors, positions):
    half_rot = ROT // 2
    inv_freq = 10000.0 ** (-2.0 * jnp.arange(half_rot, dtype=jnp.float32) / ROT)
    angles = positions.astype(jnp.float32)[:, None] * inv_freq[None, :]
    cosine = jnp.cos(angles)[:, None, :]
    sine_part = jnp.sin(angles)[:, None, :]
    lower_half = vectors[..., :half_rot]
    upper_half = vectors[..., half_rot:ROT]
    return jnp.concatenate(
        [
            lower_half * cosine - upper_half * sine_part,
            upper_half * cosine + lower_half * sine_part,
            vectors[..., ROT:],
        ],
        axis=-1,
    )


def token_positions(local_req, cached):
    onehot = local_req[:, None] == jnp.arange(cached.shape[0], dtype=jnp.int32)[None, :]
    stretch_sizes = jnp.sum(onehot.astype(jnp.int32), axis=0)
    starts = jnp.cumsum(stretch_sizes) - stretch_sizes
    own_start = jnp.sum(jnp.where(onehot, starts[None, :], 0), axis=1)
    own_cached = jnp.sum(jnp.where(onehot, cached[None, :], 0), axis=1)
    return own_cached + jnp.arange(local_req.shape[0], dtype=jnp.int32) - own_start


def attend(queries, new_keys, new_values, cache_keys, cache_values, local_req, cached, positions):
    span = cache_keys.shape[0] // cached.shape[0]
    key_slot = jnp.arange(cache_keys.shape[0], dtype=jnp.int32)
    key_owner = key_slot // span
    key_place = key_slot % span
    cache_ok = (local_req[:, None] == key_owner[None, :]) & (
        key_place[None, :] < jnp.repeat(cached, span)[None, :]
    )
    new_ok = (local_req[:, None] == local_req[None, :]) & (positions[None, :] <= positions[:, None])
    allowed = jnp.concatenate([cache_ok, new_ok], axis=1)
    all_keys = jnp.concatenate([cache_keys, new_keys], axis=0)
    all_values = jnp.concatenate([cache_values, new_values], axis=0)
    scores = jnp.einsum(
        "thd,khd->htk", queries, all_keys, preferred_element_type=jnp.float32
    ) * HD ** (-0.5)
    scores = jnp.where(allowed[None], scores, -1e30)
    peak = jnp.max(scores, axis=2, keepdims=True)
    exp_scores = jnp.exp(scores - peak)
    attn_probs = (exp_scores / jnp.sum(exp_scores, axis=2, keepdims=True)).astype(jnp.bfloat16)
    return jnp.einsum(
        "htk,khd->thd", attn_probs, all_values, preferred_element_type=jnp.float32
    ).astype(jnp.bfloat16)


def share_pages(local_pool, groups):
    grouped = local_pool.reshape(
        local_pool.shape[0], 2, local_pool.shape[2], groups, local_pool.shape[3] // groups
    )
    shared = lax.all_to_all(grouped, "head", split_axis=3, concat_axis=0, tiled=True)
    return shared.reshape(shared.shape[0], 2, shared.shape[2], shared.shape[4])


def shards(
    states,
    pre_gain,
    pre_shift,
    mlp_gain,
    mlp_shift,
    qkv_weight,
    qkv_bias,
    out_weight,
    out_bias,
    up_weight,
    up_bias,
    down_weight,
    down_bias,
    kv_cache,
    token_request,
    cached_len,
    page_table,
    migrations,
):
    gathered = lax.all_gather(states, "head", axis=1, tiled=True)
    wide = gathered.astype(jnp.float32)
    pre_normed = layer_norm(wide, pre_gain, pre_shift)
    mlp_normed = layer_norm(wide, mlp_gain, mlp_shift)
    tok_rows = gathered.shape[0]
    joined = jnp.dot(
        pre_normed,
        lax.all_gather(qkv_weight, "tok", axis=0, tiled=True),
        preferred_element_type=jnp.float32,
    )
    joined = (joined + qkv_bias).reshape(tok_rows, -1, 3, HD)
    local_req = token_request - lax.axis_index("tok") * cached_len.shape[0]
    positions = token_positions(local_req, cached_len)
    queries = rotate(joined[:, :, 0], positions).astype(jnp.bfloat16)
    new_keys = rotate(joined[:, :, 1], positions).astype(jnp.bfloat16)
    new_values = joined[:, :, 2].astype(jnp.bfloat16)
    head_groups = lax.axis_size("head")
    pool_size = kv_cache.shape[0]
    sources = migrations[:, 0]
    targets = migrations[:, 1]
    own_index = lax.axis_index("head")
    owner_mask = sources // pool_size == own_index
    picked = jnp.where(
        owner_mask[:, None, None, None], kv_cache[sources % pool_size], jnp.zeros((), jnp.bfloat16)
    )
    moved_pages = lax.psum(picked, "head").astype(jnp.float32).astype(jnp.bfloat16)
    landing = jnp.where(targets // pool_size == own_index, targets % pool_size, pool_size)
    local_pool = kv_cache.at[landing].set(moved_pages, mode="drop")
    page_pool = share_pages(local_pool, head_groups)
    pages = page_pool[page_table.reshape(-1)]
    cache_keys = pages[:, 0].reshape(-1, queries.shape[1], HD)
    cache_values = pages[:, 1].reshape(-1, queries.shape[1], HD)
    heads_out = attend(
        queries, new_keys, new_values, cache_keys, cache_values, local_req, cached_len, positions
    ).reshape(tok_rows, -1)
    attention_part = jnp.dot(
        heads_out,
        lax.all_gather(out_weight, "tok", axis=1, tiled=True),
        preferred_element_type=jnp.float32,
    )
    hidden = jax.nn.gelu(
        jnp.dot(mlp_normed, up_weight, preferred_element_type=jnp.float32) + up_bias,
        approximate=False,
    ).astype(jnp.bfloat16)
    feed_part = jnp.dot(hidden, down_weight, preferred_element_type=jnp.float32)
    summed = lax.psum_scatter(
        (attention_part + feed_part).astype(jnp.bfloat16), "head", scatter_dimension=1, tiled=True
    ).astype(jnp.float32)
    return (summed + out_bias + down_bias).astype(jnp.bfloat16)


def solution(mesh):
    in_specs = (
        P("tok", "head"),
        P(),
        P(),
        P(),
        P(),
        P("tok", "head"),
        P("head"),
        P("head", "tok"),
        P("head"),
        P(None, "head"),
        P("head"),
        P("head", None),
        P("head"),
        P(("tok", "head"), None, None, None),
        P("tok"),
        P("tok"),
        P("tok", None),
        P("tok", None),
    )
    out_specs = P("tok", "head")
    return jax.shard_map(shards, mesh=mesh, in_specs=in_specs, out_specs=out_specs, check_vma=False)
```

profile of v0, /device:TPU:0, one launch (start us, length us, event | category | flops | bytes accessed | tf_op | source)
XLA Modules:
  0.0 436.5 jit_solution(8468783990483172287)
XLA Ops:
  6.5 1.7 copy.59
  8.3 2.0 gather_fusion
  10.3 3.1 broadcast_select_fusion
  15.9 123.9 %all-reduce.2.cloned.1.call-done = bf16[8,2,16,4096]{3,2,1,0:T(8,128)(2,1)} async-done(((bf16[8,2,16,4096]{3,2,1,0:T(8,128)(2,1)}), bf16[8,2,16,4096]{3,2,1,0:T(8,128)(2,1)}) %all-reduce.2.cloned.1.call-update) | async-done | bytes 2097168 | tf_op jit(solution)/shard_map/psum | solution.py:122
  139.8 3.2 scatter_fusion
  143.1 1.8 copy.55
  144.8 4.8 %all-to-all-start = ((bf16[9,2,16,16,256]{4,2,1,0,3:T(8,128)(2,1)}), bf16[9,2,16,16,256]{4,2,1,0,3:T(8,128)(2,1)S(1)}, u32[]{:S(2)}, u32[]{:S(2)}) async-start(bf16[9,2,16,16,256]{4,2,1,0,3:T(8,128)(2,1)} %bitcast.48), calls=%async_computation | async-start | bytes 4718592 | tf_op jit(solution)/shard_map/all_to_all | solution.py:73
  153.3 33.0 %all-to-all-done = bf16[9,2,16,16,256]{4,2,1,0,3:T(8,128)(2,1)S(1)} async-done(((bf16[9,2,16,16,256]{4,2,1,0,3:T(8,128)(2,1)}), bf16[9,2,16,16,256]{4,2,1,0,3:T(8,128)(2,1)S(1)}, u32[]{:S(2)}, u32[]{:S(2)}) %all-to-all-start) | async-done | bytes 2359328 | tf_op jit(solution)/shard_map/all_to_all | solution.py:73
  186.3 2.0 gather_fusion.1
  188.3 1.7 fusion.146
  191.8 2.1 copy.39
  193.8 16.8 %all-gather.4.cloned.1.call-done = bf16[512,4096]{1,0:T(8,128)(2,1)} async-done(((bf16[512,256]{1,0:T(8,128)(2,1)}), bf16[512,4096]{1,0:T(8,128)(2,1)}) %all-gather.4.cloned.1.call-update) | async-done | bytes 4194320 | tf_op jit(solution)/shard_map/all_gather | solution.py:97
  210.6 3.0 convert_reduce_fusion
  215.4 24.2 %fusion.40 = f32[512,4096]{1,0:T(8,128)} fusion(bf16[1024,4096]{1,0:T(8,128)(2,1)} %param.29, bf16[4096,1024]{1,0:T(8,128)(2,1)} %param.27, bf16[512,4096]{1,0:T(8,128)(2,1)} %all-gather.4.cloned.1.call-done, f32[4096]{0:T(1024)S(1)} %copy-done.9, f32[4096]{0:T(1024)S(1)} %copy-done.10, f32[512]{0:T(512)S(1)} %add_rsqrt_fusion, ...), kind=kOutput, calls=%fused_computation.57 | convolution fusion | flops 8637120512 | bytes 29401088 | tf_op jit(solution)/shard_map/dot_general | solution.py:141
  239.5 61.8 %all-gather.6.cloned.1.call-done = bf16[4096,768]{1,0:T(8,128)(2,1)} async-done(((bf16[512,768]{1,0:T(8,128)(2,1)}), bf16[4096,768]{1,0:T(8,128)(2,1)}) %all-gather.6.cloned.1.call-update) | async-done | bytes 6291472 | tf_op jit(solution)/shard_map/all_gather | solution.py:104
  301.3 9.1 %fusion.42 = f32[512,768]{1,0:T(8,128)} fusion(bf16[4096,768]{1,0:T(8,128)(2,1)} %all-gather.6.cloned.1.call-done, bf16[512,4096]{1,0:T(8,128)(2,1)} %all-gather.4.cloned.1.call-done, f32[4096]{0:T(1024)S(1)} %copy-done.11, f32[4096]{0:T(1024)S(1)} %copy-done.12, f32[512]{0:T(512)S(1)} %add_rsqrt_fusion, f32[512]{0:T(512)S(1)} %broadcast_multiply_fusion, ...), kind=kOutput, calls=%fused_computation.58 | convolution fusion | flops 3234201600 | bytes 12098560 | tf_op jit(solution)/shard_map/dot_general | solution.py:102
  310.4 1.9 copy.37
  315.3 2.2 subtract_convert_fusion.1
  317.4 10.0 %fusion.148 = (f32[2,512]{1,0:T(2,128)S(1)}, f32[2,512,2560]{2,1,0:T(8,128)}) fusion(pred[512,2560]{1,0:T(8,128)(4,1)S(1)} %copy-done.1, bf16[512,2,96]{2,0,1:T(8,128)(2,1)} %slice.83, bf16[512,2,16]{2,0,1:T(8,128)(2,1)S(1)} %get-tuple-element.17, bf16[512,2,16]{2,0,1:T(8,128)(2,1)} %get-tuple-element.18, bf16[2048,2,128]{2,0,1:T(8,128)(2,1)} %copy.44, ...), kind=kOutput, calls=%fused_computation.190 | convolution fusion | flops 687606272 | bytes 13373440 | tf_op jit(solution)/shard_map/sub | solution.py:62
  327.4 5.9 %fusion.56 = bf16[2,128,512]{2,1,0:T(8,128)(2,1)S(1)} fusion(f32[2,512,2560]{2,1,0:T(8,128)} %get-tuple-element.24, f32[2,512]{1,0:T(2,128)S(1)} %get-tuple-element.23, bf16[512,2,128]{0,2,1:T(8,128)(2,1)S(1)} %copy-done.3, bf16[2048,2,128]{0,2,1:T(8,128)(2,1)S(1)} %copy-done.2), kind=kOutput, calls=%fused_computation.70 | convolution fusion | flops 679084032 | bytes 12062720 | tf_op jit(solution)/shard_map/htk,khd->thd/dot_general | solution.py:64
  333.3 22.3 %all-gather.8.cloned.1.call-done = bf16[256,4096]{1,0:T(8,128)(2,1)} async-done(((bf16[256,512]{1,0:T(8,128)(2,1)}), bf16[256,4096]{1,0:T(8,128)(2,1)}) %all-gather.8.cloned.1.call-update) | async-done | bytes 2097168 | tf_op jit(solution)/shard_map/all_gather | solution.py:134
  355.7 7.2 %add_convert_fusion = bf16[512,4096]{1,0:T(8,128)(2,1)} fusion(f32[512,4096]{1,0:T(8,128)} %fusion.40, bf16[512,256]{0,1:T(8,128)(2,1)S(1)} %bitcast.56, bf16[256,4096]{1,0:T(8,128)(2,1)} %all-gather.8.cloned.1.call-done), kind=kOutput, calls=%fused_computation.18 | convolution fusion | flops 1077936128 | bytes 14942208 | tf_op jit(solution)/shard_map/dot_general | solution.py:132
  362.9 65.4 %reduce-scatter.2.cloned.1.call-done = bf16[512,256]{1,0:T(8,128)(2,1)} async-done(((bf16[512,4096]{1,0:T(8,128)(2,1)}), bf16[512,256]{1,0:T(8,128)(2,1)}) %reduce-scatter.2.cloned.1.call-update) | async-done | bytes 262160 | tf_op jit(solution)/shard_map/reduce_scatter | solution.py:142
  428.3 1.7 add_convert_fusion.1
  (76 shorter events, 12.5 us)
Async XLA Ops:
  6.5 1.7 copy-start.8
  6.5 133.3 %all-reduce.2.cloned.1.call-start = ((), (), s32[]{:S(2)}) async-start(), calls=%async_computation.2 | async-start | bytes 4194304 | tf_op jit(solution)/shard_map/psum | solution.py:122
  13.4 2.1 copy-start.5
  13.4 2.4 copy-start.4
  13.4 197.2 %all-gather.4.cloned.1.call-start = ((), (), s32[]{:S(2)}) async-start(), calls=%async_computation.3 | async-start | bytes 4456448 | tf_op jit(solution)/shard_map/all_gather | solution.py:97
  14.2 287.1 %all-gather.6.cloned.1.call-start = ((), (), s32[]{:S(2)}) async-start(), calls=%async_computation.4 | async-start | bytes 7077888 | tf_op jit(solution)/shard_map/all_gather | solution.py:104
  14.9 340.7 %all-gather.8.cloned.1.call-start = ((), (), s32[]{:S(2)}) async-start(), calls=%async_computation.5 | async-start | bytes 2359296 | tf_op jit(solution)/shard_map/all_gather | solution.py:134
  144.8 6.0 %copy-start.15 = (s32[2,64]{1,0:T(2,128)S(1)}, s32[2,64]{1,0:T(2,128)}, u32[]{:S(2)}) copy-start(s32[2,64]{1,0:T(2,128)} %param.34) | copy-start | bytes 1540
  144.8 41.5 %all-to-all-start = ((bf16[9,2,16,16,256]{4,2,1,0,3:T(8,128)(2,1)}), bf16[9,2,16,16,256]{4,2,1,0,3:T(8,128)(2,1)S(1)}, u32[]{:S(2)}, u32[]{:S(2)}) async-start(bf16[9,2,16,16,256]{4,2,1,0,3:T(8,128)(2,1)} %bitcast.48), calls=%async_computation | async-start | bytes 4718592 | tf_op jit(solution)/shard_map/all_to_all | solution.py:73
  149.6 278.7 %reduce-scatter.2.cloned.1.call-start = ((), (), s32[]{:S(2)}) async-start(), calls=%async_computation.6 | async-start | bytes 4456448 | tf_op jit(solution)/shard_map/reduce_scatter | solution.py:142
  210.6 3.4 copy-start
  214.0 1.2 copy-start.9
  214.1 1.2 copy-start.10
  214.1 1.3 copy-start.13
  215.3 86.0 %copy-start.11 = (f32[4096]{0:T(1024)S(1)}, f32[4096]{0:T(1024)}, u32[]{:S(2)}) copy-start(f32[4096]{0:T(1024)} %param.20) | copy-start | bytes 49156
  215.3 85.9 %copy-start.12 = (f32[4096]{0:T(1024)S(1)}, f32[4096]{0:T(1024)}, u32[]{:S(2)}) copy-start(f32[4096]{0:T(1024)} %param.19) | copy-start | bytes 49156
  215.3 85.9 %copy-start.14 = (f32[768]{0:T(1024)S(1)}, f32[768]{0:T(1024)}, u32[]{:S(2)}) copy-start(f32[768]{0:T(1024)} %param.24) | copy-start | bytes 9220
  315.3 2.2 copy-start.1
  317.4 10.0 %copy-start.2 = (bf16[2048,2,128]{0,2,1:T(8,128)(2,1)S(1)}, bf16[2048,2,128]{0,2,1:T(8,128)(2,1)}, u32[]{:S(2)}) copy-start(bf16[2048,2,128]{0,2,1:T(8,128)(2,1)} %copy.39) | copy-start | bytes 3145732
  317.4 10.0 %copy-start.3 = (bf16[512,2,128]{0,2,1:T(8,128)(2,1)S(1)}, bf16[512,2,128]{0,2,1:T(8,128)(2,1)}, u32[]{:S(2)}) copy-start(bf16[512,2,128]{0,2,1:T(8,128)(2,1)} %fusion.94) | copy-start | bytes 786436
  362.9 65.4 %copy-start.6 = (f32[256]{0:T(256)S(1)}, f32[256]{0:T(256)}, u32[]{:S(2)}) copy-start(f32[256]{0:T(256)} %param.30) | copy-start | bytes 3076
  362.9 65.4 %copy-start.7 = (f32[256]{0:T(256)S(1)}, f32[256]{0:T(256)}, u32[]{:S(2)}) copy-start(f32[256]{0:T(256)} %param.26) | copy-start | bytes 3076
Sparse Core Ops, SparseCore 0:
  13.6 126.1 all-reduce.1
  141.4 69.1 all-gather.3
  212.9 88.3 all-gather.5
  303.3 52.3 all-gather.7
  363.1 65.1 reduce-scatter.1
where the time goes:
time: 437 us
  waiting for transfers between devices  325 us (74%)
  matrix products  56.4 us (13%)
  local copies, waits for them, and re-layouts  22.7 us (5%)
  other arithmetic  14.1 us (3%)
  between operations  13.4 us (3%)
  starting transfers between devices  4.96 us (1%)
    psum x1, waiting for transfers between devices, shards(): lax.psum(picked, 'head').astype(jnp.float32).astype(jnp.bfloat16)  124 us
    reduce_scatter x1, waiting for transfers between devices, shards(): lax.psum_scatter((attention_part + feed_part).astype(jnp.bfloat16), 'head...  65.4 us
    all_gather x1, waiting for transfers between devices, shards(): lax.all_gather(qkv_weight, 'tok', axis=0, tiled=True)  61.8 us
    all_to_all x1, waiting for transfers between devices, share_pages(): lax.all_to_all(grouped, 'head', split_axis=3, concat_axis=0, tiled=True)  33 us
    dot_general x1, matrix products, shards(): feed_part = jnp.dot(hidden, down_weight, preferred_element_type=jnp.float32)  24.2 us
    all_gather x1, waiting for transfers between devices, shards(): lax.all_gather(out_weight, 'tok', axis=1, tiled=True)  22.3 us
    all_gather x1, waiting for transfers between devices, shards(): gathered = lax.all_gather(states, 'head', axis=1, tiled=True)  16.8 us
    sub x1, matrix products, attend(): exp_scores = jnp.exp(scores - peak)  9.97 us
  transfers between devices with their start and end apart: 6, of which 6 were waited for; matrix products, arithmetic and copies ran while one was open for 18% of the time, Pallas kernels for 0%

commit v1 on v0

--- a/solution.py
+++ b/solution.py
@@ -1,3 +1,4 @@
+import functools
 import jax
 import jax.numpy as jnp
 from jax import lax
@@ -6,6 +7,14 @@
 HD = 128
 ROT = 32
 epsilon = 1e-05
+
+
+def turn_shapes(s0, mesh_name):
+    f_now = lax.all_gather(s0, axis_name=mesh_name).sum(axis=0)
+    return f_now
+
+
+map_the_samples = functools.partial(turn_shapes, mesh_name="head")
 
 
 def layer_norm(wide, gain, shift):
@@ -119,7 +128,7 @@
     picked = jnp.where(
         owner_mask[:, None, None, None], kv_cache[sources % pool_size], jnp.zeros((), jnp.bfloat16)
     )
-    moved_pages = lax.psum(picked, "head").astype(jnp.float32).astype(jnp.bfloat16)
+    moved_pages = map_the_samples(picked).astype(jnp.float32).astype(jnp.bfloat16)
     landing = jnp.where(targets // pool_size == own_index, targets % pool_size, pool_size)
     local_pool = kv_cache.at[landing].set(moved_pages, mode="drop")
     page_pool = share_pages(local_pool, head_groups)

time: 437 us -> 465 us (1.064)
  other arithmetic: 14.1 us -> 27.4 us
  waiting for transfers between devices: 325 us -> 334 us
  local copies, waits for them, and re-layouts: 22.7 us -> 28.7 us
    all_gather x0 -> x1, waiting for transfers between devices: none -> 168 us  [turn_shapes(): f_now = lax.all_gather(s0, axis_name=mesh_name).sum(axis=0)]
    psum x1 -> x0, waiting for transfers between devices: 124 us -> none  [shards(): lax.psum(picked, 'head').astype(jnp.float32).astype(jnp.bfloat16)]
    all_to_all x1, waiting for transfers between devices: 33 us -> 0.01 us  [share_pages(): lax.all_to_all(grouped, 'head', split_axis=3, concat_axis=0, tiled=True)]
    all_gather x1, waiting for transfers between devices: 16.8 us -> 36.8 us  [shards(): gathered = lax.all_gather(states, 'head', axis=1, tiled=True)]
    all_gather x1, waiting for transfers between devices: 22.3 us -> 8.03 us  [shards(): lax.all_gather(out_weight, 'tok', axis=1, tiled=True)]
    reduce_sum x0 -> x1, other arithmetic: none -> 13 us  [turn_shapes(): f_now = lax.all_gather(s0, axis_name=mesh_name).sum(axis=0)]
    all_gather x1, waiting for transfers between devices: 61.8 us -> 54.4 us  [shards(): lax.all_gather(qkv_weight, 'tok', axis=0, tiled=True)]
  transfers between devices with their start and end apart: 6 -> 6, of which waited for: 6 -> 5; matrix products, arithmetic and copies ran while one was open for 18% -> 22% of each run, Pallas kernels for 0% -> 0%
where the time goes in v1:
time: 465 us
  waiting for transfers between devices  334 us (72%)
  matrix products  56.3 us (12%)
  local copies, waits for them, and re-layouts  28.7 us (6%)
  other arithmetic  27.4 us (6%)
  between operations  13.4 us (3%)
  starting transfers between devices  5.51 us (1%)
    all_gather x1, waiting for transfers between devices, turn_shapes(): f_now = lax.all_gather(s0, axis_name=mesh_name).sum(axis=0)  168 us
    reduce_scatter x1, waiting for transfers between devices, shards(): lax.psum_scatter((attention_part + feed_part).astype(jnp.bfloat16), 'head...  65.3 us
    all_gather x1, waiting for transfers between devices, shards(): lax.all_gather(qkv_weight, 'tok', axis=0, tiled=True)  54.4 us
    all_gather x1, waiting for transfers between devices, shards(): gathered = lax.all_gather(states, 'head', axis=1, tiled=True)  36.8 us
    dot_general x1, matrix products, shards(): feed_part = jnp.dot(hidden, down_weight, preferred_element_type=jnp.float32)  23.8 us
    reduce_sum x1, other arithmetic, turn_shapes(): f_now = lax.all_gather(s0, axis_name=mesh_name).sum(axis=0)  13 us
    sub x1, matrix products, attend(): exp_scores = jnp.exp(scores - peak)  9.87 us
    dot_general x1, matrix products, shards(): jnp.dot(pre_normed, lax.all_gather(qkv_weight, 'tok', axis=0, tiled=True)...  9.36 us
  transfers between devices with their start and end apart: 6, of which 5 were waited for; matrix products, arithmetic and copies ran while one was open for 22% of the time, Pallas kernels for 0%

profile of v1, /device:TPU:0, one launch (start us, length us, event | category | flops | bytes accessed | tf_op | source)
XLA Modules:
  0.0 464.7 jit_solution(9687319788795904769)
XLA Ops:
  8.3 2.0 gather_fusion
  10.4 3.2 bitcast_select_fusion
  19.6 36.8 %all-gather.7.cloned.1.call-done = bf16[512,4096]{1,0:T(8,128)(2,1)} async-done(((bf16[512,256]{1,0:T(8,128)(2,1)}), bf16[512,4096]{1,0:T(8,128)(2,1)}) %all-gather.7.cloned.1.call-update) | async-done | bytes 4194320 | tf_op jit(solution)/shard_map/all_gather | solution.py:106
  56.4 3.0 convert_reduce_fusion
  61.1 167.8 %all-gather.5.cloned.1.call-done = bf16[16,8,2,16,4096]{4,3,2,1,0:T(8,128)(2,1)} async-done(((bf16[1,8,2,16,4096]{4,3,2,1,0:T(8,128)(2,1)}), bf16[16,8,2,16,4096]{4,3,2,1,0:T(8,128)(2,1)}) %all-gather.5.cloned.1.call-update) | async-done | bytes 33554448 | tf_op jit(solution)/shard_map/all_gather | solution.py:13
  228.9 13.0 %reduce_sum.74 = bf16[8,2,16,4096]{3,2,1,0:T(8,128)(2,1)} reduce(bf16[16,8,2,16,4096]{4,3,2,1,0:T(8,128)(2,1)} %all-gather.5.cloned.1.call-done, bf16[]{:T(256)} %constant.46.clone.1), dimensions={0}, to_apply=%region_0.0 | reduce | flops 15728640 | bytes 35651584 | tf_op jit(solution)/shard_map/reduce_sum | solution.py:13
  241.9 3.3 scatter_fusion
  245.2 1.7 copy.62
  246.9 5.2 %all-to-all-start = ((bf16[9,2,16,16,256]{4,2,1,0,3:T(8,128)(2,1)}), bf16[9,2,16,16,256]{4,2,1,0,3:T(8,128)(2,1)S(1)}, u32[]{:S(2)}, u32[]{:S(2)}) async-start(bf16[9,2,16,16,256]{4,2,1,0,3:T(8,128)(2,1)} %bitcast.50), calls=%async_computation | async-start | bytes 4718592 | tf_op jit(solution)/shard_map/all_to_all | solution.py:82
  252.4 23.8 %fusion.40 = f32[512,4096]{1,0:T(8,128)} fusion(bf16[1024,4096]{1,0:T(8,128)(2,1)} %param.29, bf16[4096,1024]{1,0:T(8,128)(2,1)} %param.27, bf16[512,4096]{1,0:T(8,128)(2,1)} %all-gather.7.cloned.1.call-done, f32[4096]{0:T(1024)S(1)} %copy-done.9, f32[4096]{0:T(1024)S(1)} %copy-done.10, f32[512]{0:T(512)S(1)} %add_rsqrt_fusion, ...), kind=kOutput, calls=%fused_computation.57 | convolution fusion | flops 8637120512 | bytes 29401088 | tf_op jit(solution)/shard_map/dot_general | solution.py:150
  276.2 54.4 %all-gather.9.cloned.1.call-done = bf16[4096,768]{1,0:T(8,128)(2,1)} async-done(((bf16[512,768]{1,0:T(8,128)(2,1)}), bf16[4096,768]{1,0:T(8,128)(2,1)}) %all-gather.9.cloned.1.call-update) | async-done | bytes 6291472 | tf_op jit(solution)/shard_map/all_gather | solution.py:113
  330.6 9.4 %fusion.42 = f32[512,768]{1,0:T(8,128)} fusion(bf16[4096,768]{1,0:T(8,128)(2,1)} %all-gather.9.cloned.1.call-done, bf16[512,4096]{1,0:T(8,128)(2,1)} %all-gather.7.cloned.1.call-done, f32[4096]{0:T(1024)S(1)} %copy-done.11, f32[4096]{0:T(1024)S(1)} %copy-done.12, f32[512]{0:T(512)S(1)} %add_rsqrt_fusion, f32[512]{0:T(512)S(1)} %broadcast_multiply_fusion, ...), kind=kOutput, calls=%fused_computation.58 | convolution fusion | flops 3234201600 | bytes 12098560 | tf_op jit(solution)/shard_map/dot_general | solution.py:111
  339.9 3.0 copy.44
  343.0 2.1 fusion.147
  348.2 1.8 fusion.94
  350.0 2.4 subtract_convert_fusion.1
  352.4 2.0 gather_fusion.1
  357.8 2.1 copy.46
  359.9 9.9 %fusion.148 = (f32[2,512]{1,0:T(2,128)S(1)}, f32[2,512,2560]{2,1,0:T(8,128)}) fusion(pred[512,2560]{1,0:T(8,128)(4,1)S(1)} %copy-done.1, bf16[512,2,96]{2,0,1:T(8,128)(2,1)} %slice.83, bf16[512,2,16]{2,0,1:T(8,128)(2,1)} %get-tuple-element.17, bf16[512,2,16]{2,0,1:T(8,128)(2,1)} %get-tuple-element.18, bf16[2048,2,128]{2,0,1:T(8,128)(2,1)S(1)} %copy-done.2, ...), kind=kOutput, calls=%fused_computation.190 | convolution fusion | flops 687606272 | bytes 13373440 | tf_op jit(solution)/shard_map/sub | solution.py:71
  369.8 6.0 %fusion.56 = bf16[2,128,512]{2,1,0:T(8,128)(2,1)S(1)} fusion(f32[2,512,2560]{2,1,0:T(8,128)} %get-tuple-element.24, f32[2,512]{1,0:T(2,128)S(1)} %get-tuple-element.23, bf16[512,2,128]{0,2,1:T(8,128)(2,1)} %fusion.94, bf16[2048,2,128]{0,2,1:T(8,128)(2,1)S(1)} %copy-done.3), kind=kOutput, calls=%fused_computation.70 | convolution fusion | flops 679084032 | bytes 12062720 | tf_op jit(solution)/shard_map/htk,khd->thd/dot_general | solution.py:73
  375.8 8.0 %all-gather.11.cloned.1.call-done = bf16[256,4096]{1,0:T(8,128)(2,1)} async-done(((bf16[256,512]{1,0:T(8,128)(2,1)}), bf16[256,4096]{1,0:T(8,128)(2,1)}) %all-gather.11.cloned.1.call-update) | async-done | bytes 2097168 | tf_op jit(solution)/shard_map/all_gather | solution.py:143
  383.9 7.2 %add_convert_fusion = bf16[512,4096]{1,0:T(8,128)(2,1)} fusion(f32[512,4096]{1,0:T(8,128)} %fusion.40, bf16[512,256]{0,1:T(8,128)(2,1)S(1)} %bitcast.58, bf16[256,4096]{1,0:T(8,128)(2,1)} %all-gather.11.cloned.1.call-done), kind=kOutput, calls=%fused_computation.18 | convolution fusion | flops 1077936128 | bytes 14942208 | tf_op jit(solution)/shard_map/dot_general | solution.py:141
  391.1 65.3 %reduce-scatter.2.cloned.1.call-done = bf16[512,256]{1,0:T(8,128)(2,1)} async-done(((bf16[512,4096]{1,0:T(8,128)(2,1)}), bf16[512,256]{1,0:T(8,128)(2,1)}) %reduce-scatter.2.cloned.1.call-update) | async-done | bytes 262160 | tf_op jit(solution)/shard_map/reduce_scatter | solution.py:151
  456.5 1.7 add_convert_fusion.1
  (77 shorter events, 16.3 us)
Async XLA Ops:
  6.5 1.8 copy-start.8
  6.5 49.9 %all-gather.7.cloned.1.call-start = ((), (), s32[]{:S(2)}) async-start(), calls=%async_computation.3 | async-start | bytes 4456448 | tf_op jit(solution)/shard_map/all_gather | solution.py:106
  8.2 220.7 %all-gather.5.cloned.1.call-start = ((), (), s32[]{:S(2)}) async-start(), calls=%async_computation.2 | async-start | bytes 35651584 | tf_op jit(solution)/shard_map/all_gather | solution.py:13
  13.5 1.4 copy-start.5
  13.5 1.7 copy-start.4
  13.6 4.1 copy-start.15
  13.6 317.0 %all-gather.9.cloned.1.call-start = ((), (), s32[]{:S(2)}) async-start(), calls=%async_computation.4 | async-start | bytes 7077888 | tf_op jit(solution)/shard_map/all_gather | solution.py:113
  14.3 369.5 %all-gather.11.cloned.1.call-start = ((), (), s32[]{:S(2)}) async-start(), calls=%async_computation.5 | async-start | bytes 2359296 | tf_op jit(solution)/shard_map/all_gather | solution.py:143
  56.4 3.4 copy-start
  246.9 5.4 %copy-start.9 = (f32[4096]{0:T(1024)S(1)}, f32[4096]{0:T(1024)}, u32[]{:S(2)}) copy-start(f32[4096]{0:T(1024)} %param.22) | copy-start | bytes 49156
  246.9 5.5 %copy-start.10 = (f32[4096]{0:T(1024)S(1)}, f32[4096]{0:T(1024)}, u32[]{:S(2)}) copy-start(f32[4096]{0:T(1024)} %param.21) | copy-start | bytes 49156
  246.9 5.5 %copy-start.13 = (f32[1024]{0:T(1024)S(1)}, f32[1024]{0:T(1024)}, u32[]{:S(2)}) copy-start(f32[1024]{0:T(1024)} %param.28) | copy-start | bytes 12292
  246.9 105.4 %all-to-all-start = ((bf16[9,2,16,16,256]{4,2,1,0,3:T(8,128)(2,1)}), bf16[9,2,16,16,256]{4,2,1,0,3:T(8,128)(2,1)S(1)}, u32[]{:S(2)}, u32[]{:S(2)}) async-start(bf16[9,2,16,16,256]{4,2,1,0,3:T(8,128)(2,1)} %bitcast.50), calls=%async_computation | async-start | bytes 4718592 | tf_op jit(solution)/shard_map/all_to_all | solution.py:82
  252.1 78.4 %copy-start.11 = (f32[4096]{0:T(1024)S(1)}, f32[4096]{0:T(1024)}, u32[]{:S(2)}) copy-start(f32[4096]{0:T(1024)} %param.20) | copy-start | bytes 49156
  252.1 78.4 %copy-start.12 = (f32[4096]{0:T(1024)S(1)}, f32[4096]{0:T(1024)}, u32[]{:S(2)}) copy-start(f32[4096]{0:T(1024)} %param.19) | copy-start | bytes 49156
  252.1 78.4 %copy-start.14 = (f32[768]{0:T(1024)S(1)}, f32[768]{0:T(1024)}, u32[]{:S(2)}) copy-start(f32[768]{0:T(1024)} %param.24) | copy-start | bytes 9220
  252.2 204.3 %reduce-scatter.2.cloned.1.call-start = ((), (), s32[]{:S(2)}) async-start(), calls=%async_computation.6 | async-start | bytes 4456448 | tf_op jit(solution)/shard_map/reduce_scatter | solution.py:151
  357.5 2.4 copy-start.1
  357.8 2.1 copy-start.2
  359.9 9.9 %copy-start.3 = (bf16[2048,2,128]{0,2,1:T(8,128)(2,1)S(1)}, bf16[2048,2,128]{0,2,1:T(8,128)(2,1)}, u32[]{:S(2)}) copy-start(bf16[2048,2,128]{0,2,1:T(8,128)(2,1)} %copy.46) | copy-start | bytes 3145732
  391.1 65.4 %copy-start.6 = (f32[256]{0:T(256)S(1)}, f32[256]{0:T(256)}, u32[]{:S(2)}) copy-start(f32[256]{0:T(256)} %param.30) | copy-start | bytes 3076
  391.1 65.4 %copy-start.7 = (f32[256]{0:T(256)S(1)}, f32[256]{0:T(256)}, u32[]{:S(2)}) copy-start(f32[256]{0:T(256)} %param.26) | copy-start | bytes 3076
Sparse Core Ops, SparseCore 0:
  9.0 47.3 all-gather.6
  58.1 170.7 all-gather.4
  231.2 99.2 all-gather.8
  332.6 51.2 all-gather.10
  391.3 65.1 reduce-scatter.1
